TPU v7x, 512 devices: a whole 4x8x8 slice. The times are simulated.
512 devices in a mesh: row: 32 (over x, z), col: 16 (over y, core).
Axes of the slice: x: 4, y: 8, z: 8, core: 2. Of those that a mesh axis runs over, the one named last changes fastest.
Arguments:
- matrix: float32 [14336, 14336], P('row', 'col'), may hold values from -3 to 3
- reflectors: float32 [1, 64, 14336], P(None, None, 'row'), may hold values from -0.09375 to 0.09375
- factors: float32 [1, 64, 64], replicated, may hold values from -0.1 to 2, as said below
Outputs:
- updated: float32 [14336, 14336], P('row', 'col')
- companions: float32 [1, 64, 14336], P(None, None, 'row')
Inputs may be any that keep to these rules, and one draw needn't show every extreme that they name: `factors`: each factor is upper triangular (zero below the diagonal) with diagonal entries between 1 and 2.
All inputs are finite; a program needn't handle non-finite values.
Results may differ from a plain program's by a relative error of at most 0.0001.
Values sent between devices are 32-bit elements; how exact they have to be, the bound alone decides.
No kernel may reach another device: no remote copies, remote signals or barrier semaphores. Data moves between devices by JAX's collectives and lax.ppermute only.
A program may use at most 64 MiB of HBM per device.

v0:
```python
import jax
import jax.numpy as jnp
from jax import lax
from jax.sharding import PartitionSpec as P


def spread(block, axis, owner):
    block = jnp.where(lax.axis_index(axis) == owner, block, jnp.zeros_like(block))
    return lax.psum(block, axis)


def contract(left_side, right_side, left_dim, right_dim):
    return lax.dot_general(
        left_side,
        right_side,
        (((left_dim,), (right_dim,)), ((), ())),
        precision=lax.Precision.HIGHEST,
        preferred_element_type=jnp.float32,
    )


def reflector_blocks(values):
    group_ratio = lax.axis_size("row") // lax.axis_size("col")
    column = lax.axis_index("col")
    pieces = []
    for offset in range(group_ratio):
        root_index = column * group_ratio + offset
        pieces.append(spread(values, "row", root_index))
    return jnp.concatenate(pieces, axis=values.ndim - 1)


def shards(matrix, reflectors, factors):
    current = matrix
    reflector_cols = reflector_blocks(reflectors)
    v_rows = reflectors[0]
    v_cols = reflector_cols[0]
    factor = factors[0]
    partial_value = contract(v_cols, current, 1, 1)
    column_partial = contract(v_rows, current, 1, 0)
    row_sums = lax.psum(partial_value, "col")
    x_rows = contract(factor, row_sums, 0, 0)
    projected = lax.psum(contract(v_rows, x_rows, 1, 1), "row")
    mixing = contract(projected, factor, 0, 0)
    w_rows = x_rows - 0.5 * contract(mixing, v_rows, 1, 0)
    col_sums = lax.psum(column_partial, "row")
    x_cols = contract(factor, col_sums, 0, 0)
    w_cols = x_cols - 0.5 * contract(mixing, v_cols, 1, 0)
    current = current - contract(v_rows, w_cols, 0, 0) - contract(w_rows, v_cols, 0, 0)
    results = [w_rows]
    return (current, jnp.stack(results))


def solution(mesh):
    return jax.shard_map(
        shards,
        mesh=mesh,
        in_specs=(P("row", "col"), P(None, None, "row"), P()),
        out_specs=(P("row", "col"), P(None, None, "row")),
        check_vma=False,
    )
```

profile of v0, /device:TPU:24, one launch (start us, length us, event | category | flops | bytes accessed | tf_op | source)
XLA Modules:
  0.0 447.1 jit_solution(9648008019465141000)
XLA Ops:
  7.2 0.0 copy-start
  7.2 0.0 copy-start.2
  7.2 0.0 copy-start.1
  7.2 0.0 all-reduce.6.cloned.1.call-start
  7.3 3.3 fusion.7
  10.6 0.0 copy-done.2
  10.6 0.7 broadcast_select_fusion.1
  11.3 0.0 all-reduce.6.cloned.1.call-update
  11.3 0.0 all-reduce.4.cloned.1.call-start
  11.4 164.7 %all-reduce.6.cloned.1.call-done = (f32[1,64,448]{2,1,0:T(8,128)}, f32[1,64,448]{2,1,0:T(8,128)}, f32[64,896]{1,0:T(8,128)}) async-done(((f32[1,64,448]{2,1,0:T(8,128)}, f32[1,64,448]{2,1,0:T(8,128)}, f32[64,896]{1,0:T(8,128)}), (f32[1,64,448]{2,1,0:T(8,128)}, f32[1,64,448]{2,1,0:T(8,128)}, f32[64,896]{1,0:T(8,128)})) %all-reduce.6.cloned.1.call-update) | async-done | bytes 458768 | tf_op jit(solution)/shard_map/psum | solution.py:9
  176.0 0.0 copy-done.1
  176.0 0.0 copy-start.3
  176.0 0.0 copy-start.4
  176.0 0.0 copy-start.6
  176.1 3.3 fusion.9
  179.4 0.0 all-reduce.4.cloned.1.call-update
  179.4 109.2 %all-reduce.4.cloned.1.call-done = f32[64,448]{1,0:T(8,128)} async-done(((f32[64,448]{1,0:T(8,128)}), f32[64,448]{1,0:T(8,128)}) %all-reduce.4.cloned.1.call-update) | async-done | bytes 114704 | tf_op jit(solution)/shard_map/psum | solution.py:40
  288.6 0.0 copy-done
  288.6 1.2 fusion.12
  289.8 0.3 convolution_bitcast_fusion.1
  290.1 143.7 %psum.39 = f32[64,64]{0,1:T(8,128)S(1)} all-reduce(f32[64,64]{0,1:T(8,128)S(1)} %convolution_bitcast_fusion.1), channel_id=1, replica_groups=mesh['row'=32,'col'=16] {'row'}, use_global_device_ids=true, to_apply=%region_4.5 | all-reduce | flops 4096 | bytes 32768 | tf_op jit(solution)/shard_map/psum | solution.py:42
  433.8 0.2 fusion.10
  434.0 0.3 fusion.2
  434.2 0.0 copy-done.3
  434.2 0.0 copy-done.4
  434.2 0.0 copy-start.5
  434.3 1.0 convolution_multiply_fusion
  435.2 0.0 copy-done.6
  435.2 0.9 fusion.1
  436.2 1.5 fusion.4
  437.6 0.0 copy-done.5
  437.6 2.6 fusion
Async XLA Ops:
  7.2 281.4 %copy-start = (f32[1,64,64]{2,1,0:T(8,128)S(1)}, f32[1,64,64]{2,1,0:T(8,128)}, u32[]{:S(2)}) copy-start(f32[1,64,64]{2,1,0:T(8,128)} %param.5) | copy-start | bytes 49156
  7.2 3.4 copy-start.2
  7.2 168.9 %copy-start.1 = (f32[448,896]{1,0:T(8,128)S(1)}, f32[448,896]{1,0:T(8,128)}, u32[]{:S(2)}) copy-start(f32[448,896]{1,0:T(8,128)} %param.3) | copy-start | bytes 4816900
  7.2 168.8 %all-reduce.6.cloned.1.call-start = ((), (), s32[]{:S(2)}) async-start(), calls=%async_computation.1 | async-start | bytes 983040 | tf_op jit(solution)/shard_map/psum | solution.py:9
  11.3 277.2 %all-reduce.4.cloned.1.call-start = ((), (), s32[]{:S(2)}) async-start(), calls=%async_computation | async-start | bytes 262144 | tf_op jit(solution)/shard_map/psum | solution.py:40
  176.0 258.2 %copy-start.3 = (f32[1,64,448]{2,1,0:T(8,128)S(1)}, f32[1,64,448]{2,1,0:T(8,128)}, u32[]{:S(2)}) copy-start(f32[1,64,448]{2,1,0:T(8,128)} %get-tuple-element.2) | copy-start | bytes 344068
  176.0 258.2 %copy-start.4 = (f32[1,64,448]{2,1,0:T(8,128)S(1)}, f32[1,64,448]{2,1,0:T(8,128)}, u32[]{:S(2)}) copy-start(f32[1,64,448]{2,1,0:T(8,128)} %get-tuple-element.3) | copy-start | bytes 344068
  176.0 259.2 %copy-start.6 = (f32[64,896]{1,0:T(8,128)S(1)}, f32[64,896]{1,0:T(8,128)}, u32[]{:S(2)}) copy-start(f32[64,896]{1,0:T(8,128)} %get-tuple-element.4) | copy-start | bytes 688132
  434.2 3.4 copy-start.5
Sparse Core Ops, SparseCore 0:
  12.3 163.7 all-reduce.5
  179.5 108.9 all-reduce.3
where the time goes:
time: 447 us
  waiting for transfers between devices  274 us (61%)
  blocking collectives  144 us (32%)
  matrix products  14.5 us (3%)
  between operations  14.2 us (3%)
    psum x1, waiting for transfers between devices, spread(): return lax.psum(block, axis)  165 us
    psum x1, blocking collectives, shards(): projected = lax.psum(contract(v_rows, x_rows, 1, 1), 'row')  144 us
    psum x1, waiting for transfers between devices, shards(): row_sums = lax.psum(partial_value, 'col')  109 us
    dot_general x10, matrix products, contract(): lax.dot_general(left_side, right_side, (((left_dim,), (right_dim,)), ((),...  14.5 us
  transfers between devices with their start and end apart: 2, of which 2 were waited for; matrix products, arithmetic and copies ran while one was open for 0% of the time, Pallas kernels for 0%

commit v1 on v0

--- a/solution.py
+++ b/solution.py
@@ -6,7 +6,7 @@
 
 def spread(block, axis, owner):
     block = jnp.where(lax.axis_index(axis) == owner, block, jnp.zeros_like(block))
-    return lax.psum(block, axis)
+    return jnp.sum(lax.all_gather(block, axis), axis=0)
 
 
 def contract(left_side, right_side, left_dim, right_dim):

time: 447 us -> 480 us (1.074)
  the two profiles are of different devices: /device:TPU:24 before, /device:TPU:8 now
where the time goes in v1:
time: 480 us
  waiting for transfers between devices  303 us (63%)
  blocking collectives  143 us (30%)
  between operations  13.9 us (3%)
  matrix products  12.9 us (3%)
  other arithmetic  6.77 us (1%)
    all_gather x2, waiting for transfers between devices, spread(): return jnp.sum(lax.all_gather(block, axis), axis=0)  181 us
    psum x1, blocking collectives, shards(): projected = lax.psum(contract(v_rows, x_rows, 1, 1), 'row')  143 us
    psum x1, waiting for transfers between devices, shards(): row_sums = lax.psum(partial_value, 'col')  106 us
    psum x1, waiting for transfers between devices, shards(): col_sums = lax.psum(column_partial, 'row')  15.7 us
    dot_general x10, matrix products, contract(): lax.dot_general(left_side, right_side, (((left_dim,), (right_dim,)), ((),...  12.9 us
  transfers between devices with their start and end apart: 4, of which 4 were waited for; matrix products, arithmetic and copies ran while one was open for 1% of the time, Pallas kernels for 0%

profile of v1, /device:TPU:8, one launch (start us, length us, event | category | flops | bytes accessed | tf_op | source)
XLA Modules:
  0.0 479.7 jit_solution(8924333056804101091)
XLA Ops:
  7.2 0.0 copy-start
  7.2 0.0 all-gather.5.cloned.1.call-start
  7.2 1.6 broadcast_select_fusion.1
  8.9 0.0 all-gather.5.cloned.1.call-update
  8.9 0.0 all-gather.7.cloned.1.call-start
  8.9 0.7 all-gather.7.cloned.1.call-update
  9.6 0.0 all-reduce.5.cloned.1.call-start
  9.7 95.1 %all-gather.5.cloned.1.call-done = f32[32,64,448]{2,1,0:T(8,128)} async-done(((f32[1,64,448]{2,1,0:T(8,128)}), f32[32,64,448]{2,1,0:T(8,128)}) %all-gather.5.cloned.1.call-update) | async-done | bytes 3670032 | tf_op jit(solution)/shard_map/all_gather | solution.py:9
  104.8 2.6 reduce.2
  107.4 0.0 copy-start.1
  107.4 85.9 %all-gather.7.cloned.1.call-done = f32[32,64,448]{2,1,0:T(8,128)} async-done(((f32[1,64,448]{2,1,0:T(8,128)}), f32[32,64,448]{2,1,0:T(8,128)}) %all-gather.7.cloned.1.call-update) | async-done | bytes 3670032 | tf_op jit(solution)/shard_map/all_gather | solution.py:9
  193.3 2.6 reduce.3
  195.9 0.0 copy-start.2
  195.9 0.0 copy-done.1
  195.9 2.3 fusion.9
  198.2 0.0 all-reduce.5.cloned.1.call-update
  198.2 0.0 all-reduce.3.cloned.1.call-start
  198.3 0.0 copy-done.2
  198.3 1.7 fusion.7
  200.0 0.0 all-reduce.3.cloned.1.call-update
  200.0 105.7 %all-reduce.5.cloned.1.call-done = f32[64,448]{1,0:T(8,128)} async-done(((f32[64,448]{1,0:T(8,128)}), f32[64,448]{1,0:T(8,128)}) %all-reduce.5.cloned.1.call-update) | async-done | bytes 114704 | tf_op jit(solution)/shard_map/psum | solution.py:40
  305.7 0.0 copy-done
  305.7 1.2 fusion.12
  306.9 0.3 convolution_bitcast_fusion.1
  307.2 142.9 %psum.23 = f32[64,64]{0,1:T(8,128)S(1)} all-reduce(f32[64,64]{0,1:T(8,128)S(1)} %convolution_bitcast_fusion.1), channel_id=1, replica_groups=mesh['row'=32,'col'=16] {'row'}, use_global_device_ids=true, to_apply=%region_4.5 | all-reduce | flops 4096 | bytes 32768 | tf_op jit(solution)/shard_map/psum | solution.py:42
  450.1 0.2 fusion.10
  450.3 1.0 convolution_multiply_fusion
  451.3 0.3 fusion.2
  451.6 0.0 copy-start.3
  451.6 15.7 %all-reduce.3.cloned.1.call-done = f32[64,896]{1,0:T(8,128)} async-done(((f32[64,896]{1,0:T(8,128)}), f32[64,896]{1,0:T(8,128)}) %all-reduce.3.cloned.1.call-update) | async-done | bytes 229392 | tf_op jit(solution)/shard_map/psum | solution.py:45
  467.2 1.8 fusion.1
  469.1 1.5 fusion.4
  470.5 0.0 copy-done.3
  470.5 2.7 fusion
Async XLA Ops:
  7.2 298.5 %copy-start = (f32[1,64,64]{2,1,0:T(8,128)S(1)}, f32[1,64,64]{2,1,0:T(8,128)}, u32[]{:S(2)}) copy-start(f32[1,64,64]{2,1,0:T(8,128)} %param.5) | copy-start | bytes 49156
  7.2 97.6 %all-gather.5.cloned.1.call-start = ((), (), s32[]{:S(2)}) async-start(), calls=%async_computation.2 | async-start | bytes 4325376 | tf_op jit(solution)/shard_map/all_gather | solution.py:9
  8.9 184.4 %all-gather.7.cloned.1.call-start = ((), (), s32[]{:S(2)}) async-start(), calls=%async_computation.3 | async-start | bytes 4325376 | tf_op jit(solution)/shard_map/all_gather | solution.py:9
  9.6 296.1 %all-reduce.5.cloned.1.call-start = ((), (), s32[]{:S(2)}) async-start(), calls=%async_computation.1 | async-start | bytes 262144 | tf_op jit(solution)/shard_map/psum | solution.py:40
  107.4 88.5 %copy-start.1 = (f32[448,896]{1,0:T(8,128)S(1)}, f32[448,896]{1,0:T(8,128)}, u32[]{:S(2)}) copy-start(f32[448,896]{1,0:T(8,128)} %param.3) | copy-start | bytes 4816900
  195.9 2.4 copy-start.2
  198.2 269.0 %all-reduce.3.cloned.1.call-start = ((), (), s32[]{:S(2)}) async-start(), calls=%async_computation | async-start | bytes 458752 | tf_op jit(solution)/shard_map/psum | solution.py:45
  451.6 19.0 %copy-start.3 = (f32[64,448]{1,0:T(8,128)}, f32[64,448]{1,0:T(8,128)S(1)}, u32[]{:S(2)}) copy-start(f32[64,448]{1,0:T(8,128)S(1)} %fusion.2) | copy-start | bytes 344068
Sparse Core Ops, SparseCore 0:
  11.8 93.0 all-gather.4
  108.6 84.6 all-gather.6
  198.4 107.2 all-reduce.4
  310.0 157.2 all-reduce.2
